TPU v7x, 512 devices: a whole 4x8x8 slice. The times are simulated.
512 devices in a mesh: frames: 64 (over x, y, core), tex: 8 (over z).
Axes of the slice: x: 4, y: 8, z: 8, core: 2. Of those that a mesh axis runs over, the one named last changes fastest.
Arguments:
- texture: bfloat16 [512, 16384], P('tex'), may hold values from -6 to 6
- requests: int32 [512, 32], P(('frames', 'tex')), may hold values from 0 to 63, as said below
- block_slot: int32 [512, 32], P(('frames', 'tex')), may hold values from 0 to 31
- texel_cell: int32 [512, 4096], P(('frames', 'tex')), may hold values from 0 to 960
- uv_frac: float32 [512, 2, 4096], P(('frames', 'tex')), may hold values from 0 to 1
- conv_weight: bfloat16 [32, 144], replicated, may hold values from -0.5 to 0.5
- cotangent: bfloat16 [512, 32, 4096], P(('frames', 'tex')), may hold values from -6 to 6
Outputs:
- rendered: bfloat16 [512, 32, 4096], P(('frames', 'tex'))
- texture_grad: float32 [512, 16384], P('tex', 'frames')
- weight_grad: float32 [32, 144], replicated
Inputs may be any that keep to these rules, and one draw needn't show every extreme that they name: The 4 tile numbers one renderer requests from one owner are distinct.
All inputs are finite; a program needn't handle non-finite values.
Results may differ from a plain program's by a relative error of at most 0.007.
Values may be sent and summed in bfloat16 or wider, within the bound.
No kernel may reach another device: no remote copies, remote signals or barrier semaphores. Data moves between devices by JAX's collectives and lax.ppermute only.
A program may use at most 64 MiB of HBM per device.

v0:
```python
import math
import jax
import jax.numpy as jnp
from jax import lax
from jax.sharding import PartitionSpec as P

CH = 16


def taps_and_weights(cell_row, frac_row, side):
    column = cell_row % (side - 1)
    row_index = cell_row // (side - 1)
    corner = row_index * side + column
    texel_taps = jnp.stack([corner, corner + 1, corner + side, corner + side + 1])
    frac_x = frac_row[0]
    frac_y = frac_row[1]
    weights = jnp.stack(
        [
            (1.0 - frac_x) * (1.0 - frac_y),
            frac_x * (1.0 - frac_y),
            (1.0 - frac_x) * frac_y,
            frac_x * frac_y,
        ]
    )
    return (texel_taps, weights)


def sample_matrix(texel_taps, weights, texel):
    positions = lax.broadcasted_iota(jnp.int32, (texel_taps.shape[1], texel), 1)
    matrix = jnp.zeros((texel_taps.shape[1], texel), jnp.float32)
    for number in range(4):
        matrix = matrix + jnp.where(
            texel_taps[number][:, None] == positions, weights[number][:, None], jnp.float32(0.0)
        )
    return matrix.astype(jnp.bfloat16)


def shifted(picture, shift_y, shift_x):
    height = picture.shape[1]
    width = picture.shape[2]
    padded_input = jnp.pad(picture, ((0, 0), (1, 1), (1, 1)))
    return padded_input[:, 1 + shift_y : 1 + shift_y + height, 1 + shift_x : 1 + shift_x + width]


def render_one(fetched, slot_row, cell_row, frac_row, conv_weight, cot_row):
    visible = fetched.shape[0]
    channels = fetched.shape[1]
    texel = fetched.shape[2]
    side = math.isqrt(texel)
    height = slot_row.shape[0]
    width = cell_row.shape[0] // height
    group_size = math.gcd(height, 16)
    group_count = height // group_size
    texel_taps, weights = taps_and_weights(cell_row, frac_row, side)
    taps_grouped = texel_taps.reshape(4, group_count, group_size * width).transpose(1, 0, 2)
    weights_grouped = weights.reshape(4, group_count, group_size * width).transpose(1, 0, 2)
    slots_grouped = slot_row.reshape(group_count, group_size)

    def forward(inputs):
        taps_part, weights_part, slots_part = inputs
        texture_lookup = sample_matrix(taps_part, weights_part, texel).reshape(
            group_size, width, texel
        )
        selected_entries = jnp.take(fetched, slots_part, axis=0)
        feature_maps = jnp.einsum(
            "qfm,qzm->qfz", selected_entries, texture_lookup, preferred_element_type=jnp.float32
        )
        return feature_maps.astype(jnp.bfloat16)

    grouped_features = lax.map(forward, (taps_grouped, weights_grouped, slots_grouped))
    feature_maps = grouped_features.transpose(2, 0, 1, 3).reshape(channels, height, width)
    offsets = [(shift_y, shift_x) for shift_y in (-1, 0, 1) for shift_x in (-1, 0, 1)]
    columns = jnp.concatenate(
        [shifted(feature_maps, shift_y, shift_x) for shift_y, shift_x in offsets], axis=0
    )
    columns = columns.reshape(9 * channels, height * width)
    preact = jnp.dot(conv_weight, columns, preferred_element_type=jnp.float32)
    sigmoid_pre = jax.nn.sigmoid(preact)
    rendered = (preact * sigmoid_pre).astype(jnp.bfloat16)
    pre_grad = (
        cot_row.astype(jnp.float32) * sigmoid_pre * (1.0 + preact * (1.0 - sigmoid_pre))
    ).astype(jnp.bfloat16)
    weight_local = jnp.einsum("op,kp->ok", pre_grad, columns, preferred_element_type=jnp.float32)
    col_grad = jnp.einsum("ok,op->kp", conv_weight, pre_grad, preferred_element_type=jnp.float32)
    col_grad = col_grad.reshape(9, channels, height, width)
    feat_grad = jnp.zeros((channels, height, width), jnp.float32)
    for number in range(9):
        shift_y, shift_x = offsets[number]
        feat_grad = feat_grad + shifted(col_grad[number], -shift_y, -shift_x)
    feat_grad = feat_grad.astype(jnp.bfloat16)
    grad_grouped = feat_grad.reshape(channels, group_count, group_size, width).transpose(1, 2, 0, 3)
    slot_numbers = jnp.arange(visible, dtype=jnp.int32)

    def backward(totals, inputs):
        taps_part, weights_part, slots_part, gradient_portion = inputs
        texture_lookup = sample_matrix(taps_part, weights_part, texel).reshape(
            group_size, width, texel
        )
        texel_gradient = jnp.einsum(
            "rzs,rsu->rzu", gradient_portion, texture_lookup, preferred_element_type=jnp.float32
        )
        selector = (slots_part[:, None] == slot_numbers[None, :]).astype(jnp.float32)
        added = jnp.einsum("gv,gct->vct", selector, texel_gradient, precision=lax.Precision.HIGHEST)
        return (totals + added, None)

    start = jnp.zeros((visible, channels, texel), jnp.float32)
    slot_grad, unused = lax.scan(
        backward, start, (taps_grouped, weights_grouped, slots_grouped, grad_grouped)
    )
    return (rendered, slot_grad.reshape(visible, channels * texel), weight_local)


def per_device(texture, requests, block_slot, texel_cell, uv_frac, conv_weight, cotangent):
    owners = lax.axis_size("tex")
    frame_count = lax.axis_size("frames")
    tile_count = texture.shape[0]
    tile_width = texture.shape[1]
    wanted_ids = requests.reshape(owners, -1)
    wanted = lax.all_to_all(wanted_ids, "tex", split_axis=0, concat_axis=0, tiled=True)
    served = jnp.take(texture, wanted.reshape(-1), axis=0).reshape(
        wanted.shape[0], wanted.shape[1], tile_width
    )
    returned_tiles = lax.all_to_all(served, "tex", split_axis=0, concat_axis=0, tiled=True)
    fetched = returned_tiles
    per_owner = fetched.shape[1]
    visible = owners * per_owner
    fetched = fetched.reshape(visible, CH, tile_width // CH)
    rendered, slot_grad, weight_local = render_one(
        fetched, block_slot[0], texel_cell[0], uv_frac[0], conv_weight, cotangent[0]
    )
    columns = tile_width // frame_count
    spread = slot_grad.reshape(visible, frame_count, columns).transpose(1, 0, 2)
    gathered = lax.all_to_all(spread, "frames", split_axis=0, concat_axis=0, tiled=True)
    gathered = gathered.reshape(frame_count, owners, per_owner, columns)
    senders = lax.all_gather(requests[0], "frames").reshape(frame_count, owners, per_owner)
    tile_numbers = jnp.arange(tile_count, dtype=jnp.int32)
    selector = (senders[None] == tile_numbers[:, None, None, None]).astype(jnp.float32)
    partial = jnp.einsum("qfoj,fojc->oqc", selector, gathered, precision=lax.Precision.HIGHEST)
    texture_grad = lax.psum_scatter(partial, "tex", scatter_dimension=0, tiled=True)
    texture_grad = texture_grad.reshape(tile_count, columns)
    norm_scale = 1.0 / math.sqrt(frame_count * owners * cotangent.shape[2])
    weight_grad = lax.psum(weight_local, ("frames", "tex")) * norm_scale
    return (rendered[None], texture_grad, weight_grad)


def solution(mesh):
    placed = (
        P("tex", None),
        P(("frames", "tex"), None),
        P(("frames", "tex"), None),
        P(("frames", "tex"), None),
        P(("frames", "tex"), None, None),
        P(),
        P(("frames", "tex"), None, None),
    )
    return jax.shard_map(
        per_device,
        mesh=mesh,
        in_specs=placed,
        out_specs=(P(("frames", "tex"), None, None), P("tex", "frames"), P()),
        check_vma=False,
    )
```

profile of v0, /device:TPU:1, one launch (start us, length us, event | category | flops | bytes accessed | tf_op | source)
XLA Modules:
  0.0 316.9 jit_solution(3174709285711801497)
XLA Ops:
  9.8 10.9 %all-to-all-start = ((s32[8,1,4]{2,1,0:T(1,128)}), s32[8,1,4]{2,1,0:T(1,128)S(1)}, u32[]{:S(2)}, u32[]{:S(2)}) async-start(s32[8,1,4]{2,1,0:T(1,128)} %bitcast.12), calls=%async_computation | async-start | bytes 8192 | tf_op jit(solution)/shard_map/all_to_all | solution.py:119
  23.1 4.1 %all-to-all-done = s32[8,1,4]{2,1,0:T(1,128)S(1)} async-done(((s32[8,1,4]{2,1,0:T(1,128)}), s32[8,1,4]{2,1,0:T(1,128)S(1)}, u32[]{:S(2)}, u32[]{:S(2)}) %all-to-all-start) | async-done | bytes 160 | tf_op jit(solution)/shard_map/all_to_all | solution.py:119
  30.5 2.7 broadcast_select_fusion
  33.3 3.6 %all-to-all-start.1 = ((bf16[8,4,16384]{2,1,0:T(4,128)(2,1)}), bf16[8,4,16384]{2,1,0:T(4,128)(2,1)S(1)}, u32[]{:S(2)}, u32[]{:S(2)}) async-start(bf16[8,4,16384]{2,1,0:T(4,128)(2,1)} %broadcast_select_fusion), calls=%async_computation.1 | async-start | bytes 2097152 | tf_op jit(solution)/shard_map/all_to_all | solution.py:123
  37.1 28.8 %all-to-all-done.1 = bf16[8,4,16384]{2,1,0:T(4,128)(2,1)S(1)} async-done(((bf16[8,4,16384]{2,1,0:T(4,128)(2,1)}), bf16[8,4,16384]{2,1,0:T(4,128)(2,1)S(1)}, u32[]{:S(2)}, u32[]{:S(2)}) %all-to-all-start.1) | async-done | bytes 1048608 | tf_op jit(solution)/shard_map/all_to_all | solution.py:123
  65.9 1.6 reshape.367
  67.5 16.0 %while.21 = (s32[]{:T(128)}, bf16[2,16,16,128]{3,2,1,0:T(8,128)(2,1)S(1)}, s32[2,16]{1,0:T(2,128)S(1)}, bf16[32,16,1024]{2,1,0:T(8,128)(2,1)}, s32[2,4,2048]{2,1...) while((s32[]{:T(128)}, ...), condition=%wide.region_1.2_spmd, body=%wide.region_0.1_spmd.sunk | while | flops 92570768 | bytes 1840141 | solution.py:70
  67.6 1.8 gather_fusion
  69.5 6.1 %fusion.57 = bf16[2,16,16,128]{3,2,1,0:T(8,128)(2,1)S(1)} fusion(bf16[2,16,16,128]{3,2,1,0:T(8,128)(2,1)S(1)} %get-tuple-element.284, s32[]{:T(128)} %get-tuple-element.283, f32[16,128]{1,0:T(8,128)S(1)} %bitcast.209, s32[16,128]{1,0:T(8,128)S(1)} %bitcast.213, f32[16,128]{1,0:T(8,128)S(1)} %bitcast.207, s32[16,128]{1,0:T(8,128)S(1)} %bitcast.211, ...), kind=kOutput, calls=%fused_computation.11.clone.1 | convolution fusion | flops 92569600 | bytes 655876 | tf_op jit(solution)/shard_map/while/body/eval_jaxpr/qfm,qzm->qfz/dot_general | solution.py:65
  75.7 1.8 gather_fusion
  77.5 6.1 %fusion.57 = bf16[2,16,16,128]{3,2,1,0:T(8,128)(2,1)S(1)} fusion(bf16[2,16,16,128]{3,2,1,0:T(8,128)(2,1)S(1)} %get-tuple-element.284, s32[]{:T(128)} %get-tuple-element.283, f32[16,128]{1,0:T(8,128)S(1)} %bitcast.209, s32[16,128]{1,0:T(8,128)S(1)} %bitcast.213, f32[16,128]{1,0:T(8,128)S(1)} %bitcast.207, s32[16,128]{1,0:T(8,128)S(1)} %bitcast.211, ...), kind=kOutput, calls=%fused_computation.11.clone.1 | convolution fusion | flops 92569600 | bytes 655876 | tf_op jit(solution)/shard_map/while/body/eval_jaxpr/qfm,qzm->qfz/dot_general | solution.py:65
  88.1 20.5 %while.22 = (s32[]{:T(128)}, f32[32,16,1024]{2,0,1:T(8,128)}, s32[2,16]{1,0:T(2,128)S(1)}, bf16[2,16,16,128]{3,2,1,0:T(8,128)(2,1)}, s32[2,4,2048]{2,1,0:T(4,128...) while((s32[]{:T(128)}, f32[32,16,1024]{2,0,1:T(8,128)}, ...), condition=%wide.region_3.4_spmd.clone, body=%wide.region_2.3_spmd.clone.sunk | while | flops 193987072 | bytes 6554495 | solution.py:107
  88.2 6.4 %fusion.61 = f32[16,16,1024]{2,1,0:T(8,128)S(1)} fusion(f32[16,128]{1,0:T(8,128)S(1)} %bitcast.217, s32[16,128]{1,0:T(8,128)S(1)} %bitcast.221, f32[16,128]{1,0:T(8,128)S(1)} %bitcast.215, s32[16,128]{1,0:T(8,128)S(1)} %bitcast.219, f32[16,128]{1,0:T(8,128)S(1)} %bitcast.216, s32[16,128]{1,0:T(8,128)S(1)} %bitcast.220, f32[16,128]{1,0:T(8,128)S(1)} %bitcast.214, ...), kind=kOutput, calls=%fused_computation.36.clone.1 | convolution fusion | flops 92274688 | bytes 1180160 | tf_op jit(solution)/shard_map/while/body/eval_jaxpr/rzs,rsu->rzu/dot_general | solution.py:99
  94.6 3.0 select_add_fusion.2
  97.6 6.4 %fusion.61 = f32[16,16,1024]{2,1,0:T(8,128)S(1)} fusion(f32[16,128]{1,0:T(8,128)S(1)} %bitcast.217, s32[16,128]{1,0:T(8,128)S(1)} %bitcast.221, f32[16,128]{1,0:T(8,128)S(1)} %bitcast.215, s32[16,128]{1,0:T(8,128)S(1)} %bitcast.219, f32[16,128]{1,0:T(8,128)S(1)} %bitcast.216, s32[16,128]{1,0:T(8,128)S(1)} %bitcast.220, f32[16,128]{1,0:T(8,128)S(1)} %bitcast.214, ...), kind=kOutput, calls=%fused_computation.36.clone.1 | convolution fusion | flops 92274688 | bytes 1180160 | tf_op jit(solution)/shard_map/while/body/eval_jaxpr/rzs,rsu->rzu/dot_general | solution.py:99
  104.0 4.5 %select_add_fusion.2 = f32[32,16,1024]{2,0,1:T(8,128)} fusion(f32[32,16,1024]{2,0,1:T(8,128)} %get-tuple-element.317, f32[16,16,1024]{2,1,0:T(8,128)S(1)} %fusion.61, pred[]{:T(512)S(6)} %compare.12, s32[16]{0:T(128)S(1)} %fusion.62), kind=kOutput, calls=%fused_computation.37.clone.1 | convolution fusion | flops 101712384 | bytes 5242945 | tf_op jit(solution)/shard_map/while/body/eval_jaxpr/gv,gct->vct/dot_general | solution.py:103
  108.6 4.1 %copy.29 = f32[32,16,1024]{2,1,0:T(8,128)} copy(f32[32,16,1024]{2,0,1:T(8,128)} %get-tuple-element.73) | data formatting | bytes 4194304 | tf_op jit(solution)/shard_map/while | solution.py:107
  112.7 2.9 reshape_reshape.3
  115.6 4.1 %copy.30 = f32[64,32,256]{2,1,0:T(8,128)} copy(f32[64,32,256]{2,0,1:T(8,128)} %bitcast.186) | data formatting | bytes 4194304 | tf_op jit(solution)/shard_map/transpose | solution.py:132
  119.7 11.1 %all-to-all-start.2 = ((f32[64,32,256]{2,1,0:T(8,128)}), f32[64,32,256]{2,1,0:T(8,128)}, u32[]{:S(2)}, u32[]{:S(2)}) async-start(f32[64,32,256]{2,1,0:T(8,128)} %copy.30), calls=%async_computation.2 | async-start | bytes 4194304 | tf_op jit(solution)/shard_map/all_to_all | solution.py:133
  130.9 77.5 %all-gather = s32[64,1,32]{2,1,0:T(1,128)S(1)} all-gather(s32[1,1,32]{2,1,0:T(1,128)S(1)} %bitcast.230), channel_id=1, replica_groups=mesh['frames'=64,'tex'=8] {'frames'}, dimensions={0}, use_global_device_ids=true | all-gather | bytes 8320 | tf_op jit(solution)/shard_map/all_gather | solution.py:135
  208.4 2.8 copy.31
  211.2 1.9 convolution_bitcast_fusion.2
  214.3 95.1 %psum.7 = f32[32,144]{1,0:T(8,128)S(1)} all-reduce(f32[32,144]{1,0:T(8,128)} %fusion.39), channel_id=1, replica_groups=mesh['frames'=64,'tex'=8] {'frames','tex'}, use_global_device_ids=true, to_apply=%region_5.6 | all-reduce | flops 4608 | bytes 36864 | tf_op jit(solution)/shard_map/psum | solution.py:142
  (85 shorter events, 15.2 us)
Async XLA Ops:
  7.2 20.7 %copy-start = (bf16[64,16384]{1,0:T(8,128)(2,1)S(1)}, bf16[64,16384]{1,0:T(8,128)(2,1)}, u32[]{:S(2)}) copy-start(bf16[64,16384]{1,0:T(8,128)(2,1)} %param.11) | copy-start | bytes 6291460
  9.8 17.3 %all-to-all-start = ((s32[8,1,4]{2,1,0:T(1,128)}), s32[8,1,4]{2,1,0:T(1,128)S(1)}, u32[]{:S(2)}, u32[]{:S(2)}) async-start(s32[8,1,4]{2,1,0:T(1,128)} %bitcast.12), calls=%async_computation | async-start | bytes 8192 | tf_op jit(solution)/shard_map/all_to_all | solution.py:119
  30.5 6.3 %copy-start.4 = (s32[1,4096]{1,0:T(1,128)S(1)}, s32[1,4096]{1,0:T(1,128)}, u32[]{:S(2)}) copy-start(s32[1,4096]{1,0:T(1,128)} %param.14) | copy-start | bytes 49156
  33.3 32.7 %all-to-all-start.1 = ((bf16[8,4,16384]{2,1,0:T(4,128)(2,1)}), bf16[8,4,16384]{2,1,0:T(4,128)(2,1)S(1)}, u32[]{:S(2)}, u32[]{:S(2)}) async-start(bf16[8,4,16384]{2,1,0:T(4,128)(2,1)} %broadcast_select_fusion), calls=%async_computation.1 | async-start | bytes 2097152 | tf_op jit(solution)/shard_map/all_to_all | solution.py:123
  83.5 0.9 copy-start.3
  83.5 1.0 copy-start.6
  84.5 1.1 copy-start.1
  119.7 11.2 %copy-start.5 = (s32[1,32]{1,0:T(1,128)S(1)}, s32[1,32]{1,0:T(1,128)}, u32[]{:S(2)}) copy-start(s32[1,32]{1,0:T(1,128)} %param.12) | copy-start | bytes 388
  119.7 88.7 %all-to-all-start.2 = ((f32[64,32,256]{2,1,0:T(8,128)}), f32[64,32,256]{2,1,0:T(8,128)}, u32[]{:S(2)}, u32[]{:S(2)}) async-start(f32[64,32,256]{2,1,0:T(8,128)} %copy.30), calls=%async_computation.2 | async-start | bytes 4194304 | tf_op jit(solution)/shard_map/all_to_all | solution.py:133
  130.8 179.2 %reduce-scatter.2.cloned.1.call-start = ((), (), s32[]{:S(2)}) async-start(), calls=%async_computation.4 | async-start | bytes 589824 | tf_op jit(solution)/shard_map/reduce_scatter | solution.py:139
  211.2 1.9 copy-start.2
Sparse Core Ops, SparseCore 0:
  213.3 29.5 reduce-scatter.1
where the time goes:
time: 318 us; the launch traced here: 317 us
  blocking collectives  173 us (54%)
  matrix products  37 us (12%)
  waiting for transfers between devices  32.9 us (10%)
  local copies, waits for them, and re-layouts  26.6 us (8%)
  starting transfers between devices  25.6 us (8%)
  between operations  14.4 us (5%)
  other arithmetic  7.69 us (2%)
    psum x1, blocking collectives, per_device(): weight_grad = lax.psum(weight_local, ('frames', 'tex')) * norm_scale  95.1 us
    all_gather x1, blocking collectives, per_device(): lax.all_gather(requests[0], 'frames')  77.5 us
    all_to_all x1, waiting for transfers between devices, per_device(): lax.all_to_all(served, 'tex', split_axis=0, concat_axis=0, tiled=True)  28.8 us
    dot_general x2, matrix products, backward(): jnp.einsum('rzs,rsu->rzu', gradient_portion, texture_lookup, preferred_el...  12.8 us
    dot_general x2, matrix products, forward(): jnp.einsum('qfm,qzm->qfz', selected_entries, texture_lookup, preferred_el...  12.1 us
    all_to_all x1, starting transfers between devices, per_device(): lax.all_to_all(spread, 'frames', split_axis=0, concat_axis=0, tiled=True)  11.1 us
    all_to_all x1, starting transfers between devices, per_device(): lax.all_to_all(wanted_ids, 'tex', split_axis=0, concat_axis=0, tiled=True)  10.9 us
    dot_general x2, matrix products, backward(): jnp.einsum('gv,gct->vct', selector, texel_gradient, precision=lax.Precisi...  7.51 us
  transfers between devices with their start and end apart: 4, of which 2 were waited for; matrix products, arithmetic and copies ran while one was open for 1% of the time, Pallas kernels for 0%

commit v1 on v0

--- a/solution.py
+++ b/solution.py
@@ -5,6 +5,11 @@
 from jax.sharding import PartitionSpec as P
 
 CH = 16
+
+
+def attach_spot(mine_x):
+    block_next = jnp.sum(jax.lax.all_gather(mine_x, ("frames", "tex")), 0)
+    return block_next
 
 
 def taps_and_weights(cell_row, frac_row, side):
@@ -139,7 +144,7 @@
     texture_grad = lax.psum_scatter(partial, "tex", scatter_dimension=0, tiled=True)
     texture_grad = texture_grad.reshape(tile_count, columns)
     norm_scale = 1.0 / math.sqrt(frame_count * owners * cotangent.shape[2])
-    weight_grad = lax.psum(weight_local, ("frames", "tex")) * norm_scale
+    weight_grad = attach_spot(weight_local) * norm_scale
     return (rendered[None], texture_grad, weight_grad)
 
 

time: 318 us -> 262 us (0.82); the launches traced: 317 us -> 257 us
  blocking collectives: 173 us -> 82.2 us
  waiting for transfers between devices: 32.9 us -> 55.1 us
  other arithmetic: 7.69 us -> 14.5 us
    psum x1 -> x0, blocking collectives: 95.1 us -> none  [per_device(): weight_grad = lax.psum(weight_local, ('frames', 'tex')) * norm_scale]
    reduce_scatter x1, waiting for transfers between devices: 0.01 us -> 21.2 us  [per_device(): lax.psum_scatter(partial, 'tex', scatter_dimension=0, tiled=True)]
    reduce_sum x0 -> x1, other arithmetic: none -> 6.74 us  [attach_spot(): block_next = jnp.sum(jax.lax.all_gather(mine_x, ('frames', 'tex')), 0)]
    all_gather x1, blocking collectives: 77.5 us -> 82.2 us  [per_device(): lax.all_gather(requests[0], 'frames')]
  transfers between devices with their start and end apart: 4 -> 5, of which waited for: 2 -> 4; matrix products, arithmetic and copies ran while one was open for 1% -> 19% of each run, Pallas kernels for 0% -> 0%
where the time goes in v1:
time: 262 us; the launch traced here: 257 us
  blocking collectives  82.2 us (31%)
  waiting for transfers between devices  55.1 us (21%)
  matrix products  38.7 us (15%)
  starting transfers between devices  25.6 us (10%)
  local copies, waits for them, and re-layouts  25.2 us (10%)
  between operations  15.8 us (6%)
  other arithmetic  14.5 us (6%)
    all_gather x1, blocking collectives, per_device(): lax.all_gather(requests[0], 'frames')  82.2 us
    all_to_all x1, waiting for transfers between devices, per_device(): lax.all_to_all(served, 'tex', split_axis=0, concat_axis=0, tiled=True)  28 us
    reduce_scatter x1, waiting for transfers between devices, per_device(): lax.psum_scatter(partial, 'tex', scatter_dimension=0, tiled=True)  21.2 us
    dot_general x2, matrix products, backward(): jnp.einsum('rzs,rsu->rzu', gradient_portion, texture_lookup, preferred_el...  14.5 us
    dot_general x2, matrix products, forward(): jnp.einsum('qfm,qzm->qfz', selected_entries, texture_lookup, preferred_el...  12.1 us
    all_to_all x1, starting transfers between devices, per_device(): lax.all_to_all(spread, 'frames', split_axis=0, concat_axis=0, tiled=True)  11.1 us
    all_to_all x1, starting transfers between devices, per_device(): lax.all_to_all(wanted_ids, 'tex', split_axis=0, concat_axis=0, tiled=True)  10.9 us
    dot_general x2, matrix products, backward(): jnp.einsum('gv,gct->vct', selector, texel_gradient, precision=lax.Precisi...  7.5 us
  transfers between devices with their start and end apart: 5, of which 4 were waited for; matrix products, arithmetic and copies ran while one was open for 19% of the time, Pallas kernels for 0%

profile of v1, /device:TPU:1, one launch (start us, length us, event | category | flops | bytes accessed | tf_op | source)
XLA Modules:
  0.0 257.3 jit_solution(11330770489928704566)
XLA Ops:
  10.6 10.9 %all-to-all-start = ((s32[8,1,4]{2,1,0:T(1,128)}), s32[8,1,4]{2,1,0:T(1,128)S(1)}, u32[]{:S(2)}, u32[]{:S(2)}) async-start(s32[8,1,4]{2,1,0:T(1,128)} %bitcast.12), calls=%async_computation | async-start | bytes 8192 | tf_op jit(solution)/shard_map/all_to_all | solution.py:124
  22.4 5.6 %all-to-all-done = s32[8,1,4]{2,1,0:T(1,128)S(1)} async-done(((s32[8,1,4]{2,1,0:T(1,128)}), s32[8,1,4]{2,1,0:T(1,128)S(1)}, u32[]{:S(2)}, u32[]{:S(2)}) %all-to-all-start) | async-done | bytes 160 | tf_op jit(solution)/shard_map/all_to_all | solution.py:124
  31.4 2.7 %broadcast_select_fusion = bf16[8,4,16384]{2,1,0:T(4,128)(2,1)} fusion(bf16[8,4,16384]{2,1,0:T(4,128)(2,1)} %gather.11, pred[8,4]{1,0:T(8,128)(4,1)S(1)} %copy.24), kind=kLoop, calls=%fused_computation.60 | loop fusion | flops 524288 | bytes 2097184 | tf_op jit(solution)/shard_map/jit(_take)/select_n | solution.py:125
  34.1 3.6 %all-to-all-start.1 = ((bf16[8,4,16384]{2,1,0:T(4,128)(2,1)}), bf16[8,4,16384]{2,1,0:T(4,128)(2,1)S(1)}, u32[]{:S(2)}, u32[]{:S(2)}) async-start(bf16[8,4,16384]{2,1,0:T(4,128)(2,1)} %broadcast_select_fusion), calls=%async_computation.1 | async-start | bytes 2097152 | tf_op jit(solution)/shard_map/all_to_all | solution.py:128
  38.8 28.0 %all-to-all-done.1 = bf16[8,4,16384]{2,1,0:T(4,128)(2,1)S(1)} async-done(((bf16[8,4,16384]{2,1,0:T(4,128)(2,1)}), bf16[8,4,16384]{2,1,0:T(4,128)(2,1)S(1)}, u32[]{:S(2)}, u32[]{:S(2)}) %all-to-all-start.1) | async-done | bytes 1048608 | tf_op jit(solution)/shard_map/all_to_all | solution.py:128
  68.4 16.0 %while.21 = (s32[]{:T(128)}, bf16[2,16,16,128]{3,2,1,0:T(8,128)(2,1)S(1)}, s32[2,16]{1,0:T(2,128)S(1)}, bf16[32,16,1024]{2,1,0:T(8,128)(2,1)}, s32[2,4,2048]{2,1...) while((s32[]{:T(128)}, ...), condition=%wide.region_1.2_spmd, body=%wide.region_0.1_spmd.sunk | while | flops 92570768 | bytes 1840149 | solution.py:75
  68.5 1.8 gather_fusion
  70.3 6.1 %fusion.57 = bf16[2,16,16,128]{3,2,1,0:T(8,128)(2,1)S(1)} fusion(bf16[2,16,16,128]{3,2,1,0:T(8,128)(2,1)S(1)} %get-tuple-element.284, s32[]{:T(128)S(6)} %copy.67, f32[16,128]{1,0:T(8,128)S(1)} %bitcast.211, s32[16,128]{1,0:T(8,128)S(1)} %bitcast.215, f32[16,128]{1,0:T(8,128)S(1)} %bitcast.209, s32[16,128]{1,0:T(8,128)S(1)} %bitcast.213, ...), kind=kOutput, calls=%fused_computation.11.clone.1 | convolution fusion | flops 92569600 | bytes 655876 | tf_op jit(solution)/shard_map/while/body/eval_jaxpr/qfm,qzm->qfz/dot_general | solution.py:70
  76.5 1.8 gather_fusion
  78.3 6.1 %fusion.57 = bf16[2,16,16,128]{3,2,1,0:T(8,128)(2,1)S(1)} fusion(bf16[2,16,16,128]{3,2,1,0:T(8,128)(2,1)S(1)} %get-tuple-element.284, s32[]{:T(128)S(6)} %copy.67, f32[16,128]{1,0:T(8,128)S(1)} %bitcast.211, s32[16,128]{1,0:T(8,128)S(1)} %bitcast.215, f32[16,128]{1,0:T(8,128)S(1)} %bitcast.209, s32[16,128]{1,0:T(8,128)S(1)} %bitcast.213, ...), kind=kOutput, calls=%fused_computation.11.clone.1 | convolution fusion | flops 92569600 | bytes 655876 | tf_op jit(solution)/shard_map/while/body/eval_jaxpr/qfm,qzm->qfz/dot_general | solution.py:70
  89.4 22.2 %while.22 = (s32[]{:T(128)}, f32[32,16,1024]{2,0,1:T(8,128)}, s32[2,16]{1,0:T(2,128)S(1)}, bf16[2,16,16,128]{3,2,1,0:T(8,128)(2,1)S(1)}, s32[2,4,2048]{2,1,0:T(4...) while((s32[]{:T(128)}, f32[32,16,1024]{2,0,1:T(8,128)}, ...), condition=%wide.region_3.4_spmd.clone, body=%wide.region_2.3_spmd.clone.sunk | while | flops 193987072 | bytes 6553995 | solution.py:112
  89.5 7.3 %fusion.61 = f32[16,16,1024]{2,1,0:T(8,128)S(1)} fusion(f32[16,128]{1,0:T(8,128)S(1)} %bitcast.219, s32[16,128]{1,0:T(8,128)S(1)} %bitcast.223, f32[16,128]{1,0:T(8,128)S(1)} %bitcast.217, s32[16,128]{1,0:T(8,128)S(1)} %bitcast.221, f32[16,128]{1,0:T(8,128)S(1)} %bitcast.218, s32[16,128]{1,0:T(8,128)S(1)} %bitcast.222, f32[16,128]{1,0:T(8,128)S(1)} %bitcast.216, ...), kind=kOutput, calls=%fused_computation.36.clone.1 | convolution fusion | flops 92274688 | bytes 1179652 | tf_op jit(solution)/shard_map/while/body/eval_jaxpr/rzs,rsu->rzu/dot_general | solution.py:104
  96.8 3.0 %select_add_fusion.2 = f32[32,16,1024]{2,0,1:T(8,128)} fusion(f32[32,16,1024]{2,0,1:T(8,128)} %get-tuple-element.317, f32[16,16,1024]{2,1,0:T(8,128)S(1)} %fusion.61, pred[]{:T(512)S(6)} %compare.12, s32[16]{0:T(128)S(1)} %fusion.62), kind=kOutput, calls=%fused_computation.37.clone.1 | convolution fusion | flops 101712384 | bytes 5242945 | tf_op jit(solution)/shard_map/while/body/eval_jaxpr/gv,gct->vct/dot_general | solution.py:108
  99.8 7.3 %fusion.61 = f32[16,16,1024]{2,1,0:T(8,128)S(1)} fusion(f32[16,128]{1,0:T(8,128)S(1)} %bitcast.219, s32[16,128]{1,0:T(8,128)S(1)} %bitcast.223, f32[16,128]{1,0:T(8,128)S(1)} %bitcast.217, s32[16,128]{1,0:T(8,128)S(1)} %bitcast.221, f32[16,128]{1,0:T(8,128)S(1)} %bitcast.218, s32[16,128]{1,0:T(8,128)S(1)} %bitcast.222, f32[16,128]{1,0:T(8,128)S(1)} %bitcast.216, ...), kind=kOutput, calls=%fused_computation.36.clone.1 | convolution fusion | flops 92274688 | bytes 1179652 | tf_op jit(solution)/shard_map/while/body/eval_jaxpr/rzs,rsu->rzu/dot_general | solution.py:104
  107.1 4.5 %select_add_fusion.2 = f32[32,16,1024]{2,0,1:T(8,128)} fusion(f32[32,16,1024]{2,0,1:T(8,128)} %get-tuple-element.317, f32[16,16,1024]{2,1,0:T(8,128)S(1)} %fusion.61, pred[]{:T(512)S(6)} %compare.12, s32[16]{0:T(128)S(1)} %fusion.62), kind=kOutput, calls=%fused_computation.37.clone.1 | convolution fusion | flops 101712384 | bytes 5242945 | tf_op jit(solution)/shard_map/while/body/eval_jaxpr/gv,gct->vct/dot_general | solution.py:108
  111.7 4.1 %copy.29 = f32[32,16,1024]{2,1,0:T(8,128)} copy(f32[32,16,1024]{2,0,1:T(8,128)} %get-tuple-element.73) | data formatting | bytes 4194304 | tf_op jit(solution)/shard_map/while | solution.py:112
  115.8 2.9 %reshape_reshape.3 = f32[32,64,256]{2,1,0:T(8,128)} reshape(f32[32,16,1024]{2,1,0:T(8,128)} %copy.29) | data formatting | bytes 4194304 | tf_op jit(solution)/shard_map/reshape;reshape | solution.py:137
  118.7 4.1 %copy.30 = f32[64,32,256]{2,1,0:T(8,128)} copy(f32[64,32,256]{2,0,1:T(8,128)} %bitcast.188) | data formatting | bytes 4194304 | tf_op jit(solution)/shard_map/transpose | solution.py:137
  122.8 11.1 %all-to-all-start.2 = ((f32[64,32,256]{2,1,0:T(8,128)}), f32[64,32,256]{2,1,0:T(8,128)}, u32[]{:S(2)}, u32[]{:S(2)}) async-start(f32[64,32,256]{2,1,0:T(8,128)} %copy.30), calls=%async_computation.2 | async-start | bytes 4194304 | tf_op jit(solution)/shard_map/all_to_all | solution.py:138
  134.0 82.2 %all-gather.1 = s32[64,1,32]{2,1,0:T(1,128)S(1)} all-gather(s32[1,1,32]{2,1,0:T(1,128)S(1)} %bitcast.232), channel_id=1, replica_groups=mesh['frames'=64,'tex'=8] {'frames'}, dimensions={0}, use_global_device_ids=true | all-gather | bytes 8320 | tf_op jit(solution)/shard_map/all_gather | solution.py:140
  216.2 2.8 %copy.31 = f32[64,32,256]{2,0,1:T(8,128)S(1)} copy(f32[64,32,256]{2,1,0:T(8,128)} %all-to-all-done.2) | data formatting | bytes 4194304 | tf_op jit(solution)/shard_map/all_to_all | solution.py:138
  219.1 1.9 convolution_bitcast_fusion.2
  221.3 6.7 %reduce_sum.9 = f32[32,144]{1,0:T(8,128)S(1)} reduce(f32[512,32,144]{2,1,0:T(8,128)} %bitcast.186, f32[]{:T(128)} %constant.93.clone.1), dimensions={0}, to_apply=%region_5.6 | reduce | flops 2354688 | bytes 9455620 | tf_op jit(solution)/shard_map/reduce_sum | solution.py:11
  228.7 21.2 %reduce-scatter.2.cloned.1.call-done = f32[1,64,256]{2,1,0:T(8,128)} async-done(((f32[8,64,256]{2,1,0:T(8,128)}), f32[1,64,256]{2,1,0:T(8,128)}) %reduce-scatter.2.cloned.1.call-update) | async-done | bytes 65552 | tf_op jit(solution)/shard_map/reduce_scatter | solution.py:144
  (86 shorter events, 15.7 us)
Async XLA Ops:
  8.0 20.7 %copy-start = (bf16[64,16384]{1,0:T(8,128)(2,1)S(1)}, bf16[64,16384]{1,0:T(8,128)(2,1)}, u32[]{:S(2)}) copy-start(bf16[64,16384]{1,0:T(8,128)(2,1)} %param.11) | copy-start | bytes 6291460
  10.6 17.3 %all-to-all-start = ((s32[8,1,4]{2,1,0:T(1,128)}), s32[8,1,4]{2,1,0:T(1,128)S(1)}, u32[]{:S(2)}, u32[]{:S(2)}) async-start(s32[8,1,4]{2,1,0:T(1,128)} %bitcast.12), calls=%async_computation | async-start | bytes 8192 | tf_op jit(solution)/shard_map/all_to_all | solution.py:124
  31.4 6.4 %copy-start.5 = (s32[1,32]{1,0:T(1,128)S(1)}, s32[1,32]{1,0:T(1,128)}, u32[]{:S(2)}) copy-start(s32[1,32]{1,0:T(1,128)} %param.13) | copy-start | bytes 388
  31.4 7.2 %copy-start.1 = (f32[1,2,4096]{2,1,0:T(2,128)S(1)}, f32[1,2,4096]{2,1,0:T(2,128)}, u32[]{:S(2)}) copy-start(f32[1,2,4096]{2,1,0:T(2,128)} %param.15) | copy-start | bytes 98308
  34.1 32.7 %all-to-all-start.1 = ((bf16[8,4,16384]{2,1,0:T(4,128)(2,1)}), bf16[8,4,16384]{2,1,0:T(4,128)(2,1)S(1)}, u32[]{:S(2)}, u32[]{:S(2)}) async-start(bf16[8,4,16384]{2,1,0:T(4,128)(2,1)} %broadcast_select_fusion), calls=%async_computation.1 | async-start | bytes 2097152 | tf_op jit(solution)/shard_map/all_to_all | solution.py:128
  37.7 183.6 %all-gather.4.cloned.1.call-start = ((), (), s32[]{:S(2)}) async-start(), calls=%async_computation.5 | async-start | bytes 16809984 | tf_op jit(solution)/shard_map/all_gather | solution.py:11
  84.4 0.9 copy-start.2
  84.4 1.0 copy-start.4
  122.8 11.2 %copy-start.3 = (s32[1,32]{1,0:T(1,128)S(1)}, s32[1,32]{1,0:T(1,128)}, u32[]{:S(2)}) copy-start(s32[1,32]{1,0:T(1,128)} %param.12) | copy-start | bytes 388
  122.8 93.4 %all-to-all-start.2 = ((f32[64,32,256]{2,1,0:T(8,128)}), f32[64,32,256]{2,1,0:T(8,128)}, u32[]{:S(2)}, u32[]{:S(2)}) async-start(f32[64,32,256]{2,1,0:T(8,128)} %copy.30), calls=%async_computation.2 | async-start | bytes 4194304 | tf_op jit(solution)/shard_map/all_to_all | solution.py:138
  133.9 115.9 %reduce-scatter.2.cloned.1.call-start = ((), (), s32[]{:S(2)}) async-start(), calls=%async_computation.4 | async-start | bytes 589824 | tf_op jit(solution)/shard_map/reduce_scatter | solution.py:144
Sparse Core Ops, SparseCore 0:
  87.7 133.5 all-gather.3
Sparse Core Ops, SparseCore 1:
  221.1 28.7 reduce-scatter.1
